TPU v7x, 256 devices: a whole 4x4x8 slice. The times are simulated.
256 devices in a mesh: seq: 32 (over y, z), tensor: 8 (over x, core).
Axes of the slice: x: 4, y: 4, z: 8, core: 2. Of those that a mesh axis runs over, the one named last changes fastest.
Arguments:
- query: bfloat16 [4096, 2048], P('seq', 'tensor')
- suffix_kv: bfloat16 [4096, 4, 2, 128], P('seq'), may hold values from -6 to 6
- segment_ids: int32 [32, 128], P('seq'), may hold values from 0 to 3, never falling along the last dimension, each value on 1 to 64 neighbouring positions
- request_prefix: int32 [32, 4], P('seq'), may hold values from 0 to 3
- prefix_kv: bfloat16 [32768, 4, 2, 128], P('seq')
- shard_prefix: int32 [32], P('seq'), may hold values from 0 to 3, as said below
- residual: bfloat16 [4096, 2048], P('seq'), may hold values from -3.2 to 3.2
- out_weight: bfloat16 [2048, 2048], P('tensor'), may hold values from -0.1875 to 0.1875
- norm_gain: float32 [2048], replicated, may hold values from 0.1 to 1.9
- expert_ids: int32 [4096, 6], P('seq'), may hold values from 0 to 63, all different within a row; in each aligned block of 128 rows (0 to 127, 128 to 255, ...) at most 24 rows name the same one
- gate_weights: float32 [4096, 6], P('seq'), may hold values from 0.05 to 0.5
- expert_in: bfloat16 [64, 2048, 2, 1408], P('seq', None, None, 'tensor'), may hold values from -0.125 to 0.125
- expert_out: bfloat16 [64, 1408, 2048], P('seq', 'tensor'), may hold values from -0.21875 to 0.21875
Outputs:
- attended: bfloat16 [4096, 2048], P('seq', 'tensor')
- layer_out: bfloat16 [4096, 2048], P('seq', 'tensor')
Inputs may be any that keep to these rules, and one draw needn't show every extreme that they name: `segment_ids`: on each seq index the segment numbers never fall along the 128 positions and every number occurs. `shard_prefix`: every prefix owns the same number of shards. `expert_ids`: each row names 6 different experts; within the 128 rows of one seq index no expert is named more than 24 times, and that count is reached.
All inputs are finite; a program needn't handle non-finite values.
Results may differ from a plain program's by a relative error of at most 0.02.
Values may be sent and summed in bfloat16 or wider, within the bound.
No kernel may reach another device: no remote copies, remote signals or barrier semaphores. Data moves between devices by JAX's collectives and lax.ppermute only.
A program may use at most 128 MiB of HBM per device.

v0:
```python
import functools

import jax
import jax.numpy as jnp
from jax import lax
from jax.experimental import pallas as pl
from jax.experimental.pallas import tpu as pltpu
from jax.sharding import PartitionSpec as P


QH = 16
KVH = 4


NEG_SHIFT = -(2.0 ** 100)
TOKEN_BLOCKS = 4
STAT_ROWS = 16


def split3(x):
    hi = x.astype(jnp.bfloat16).astype(jnp.float32)
    rest = x - hi
    mid = rest.astype(jnp.bfloat16).astype(jnp.float32)
    lo = (rest - mid).astype(jnp.bfloat16).astype(jnp.float32)
    return hi, mid, lo


def shard_kernel(flag_ref, q_ref, k_ref, v_ref, o_ref, *, score_scale):
    step = pl.program_id(0)
    blocks, padded_rows, width = q_ref.shape
    rows = padded_rows - 1
    stat_rows = o_ref.shape[2] - rows
    owner = flag_ref[flag_ref.shape[0] - 1].astype(jnp.float32)
    kind = lax.broadcasted_iota(jnp.int32, (stat_rows, width), 0)
    blank = jnp.where(kind == 0, NEG_SHIFT, 0.0)
    for i in range(blocks):
        present = flag_ref[step * blocks + i] > 0

        @pl.when(present)
        def _():
            scores = (
                lax.dot_general(
                    q_ref[i, :rows, :], k_ref[...], (((1,), (1,)), ((), ())),
                    preferred_element_type=jnp.float32,
                )
                * score_scale
            )
            shift = jnp.max(scores, axis=1, keepdims=True)
            weights = jnp.exp(scores - shift)
            total = jnp.sum(weights, axis=1, keepdims=True)
            gathered = jnp.dot(
                weights.astype(jnp.bfloat16), v_ref[...], preferred_element_type=jnp.float32
            )
            o_ref[i, 0, :rows, :] = gathered.astype(jnp.bfloat16)
            lane = lax.broadcasted_iota(jnp.int32, (rows, width), 1)
            table = jnp.zeros((rows, width), jnp.float32)
            for col, part in enumerate(split3(shift) + split3(total)):
                table = jnp.where(lane == col, part, table)
            table = jnp.transpose(table)[:stat_rows, :]
            matching = q_ref[i, rows:, :].astype(jnp.float32) == owner
            o_ref[i, 0, rows:, :] = jnp.where(matching, table, blank).astype(jnp.bfloat16)

        @pl.when(jnp.logical_not(present))
        def _():
            o_ref[i, 0, :rows, :] = jnp.zeros((rows, width), jnp.bfloat16)
            o_ref[i, 0, rows:, :] = blank.astype(jnp.bfloat16)


def shard_attention(flags, gathered_q, keys, values, score_scale):
    sources, padded_rows, head_size = gathered_q.shape
    rows = padded_rows - 1
    tb = TOKEN_BLOCKS
    kernel = functools.partial(shard_kernel, score_scale=score_scale)
    grid_spec = pltpu.PrefetchScalarGridSpec(
        num_scalar_prefetch=1,
        grid=(sources // tb,),
        in_specs=[
            pl.BlockSpec((tb, padded_rows, head_size), lambda b, f: (b, 0, 0)),
            pl.BlockSpec(keys.shape, lambda b, f: (0, 0)),
            pl.BlockSpec(values.shape, lambda b, f: (0, 0)),
        ],
        out_specs=pl.BlockSpec((tb, 1, rows + STAT_ROWS, head_size), lambda b, f: (b, 0, 0, 0)),
    )
    return pl.pallas_call(
        kernel,
        grid_spec=grid_spec,
        out_shape=jax.ShapeDtypeStruct((sources, 1, rows + STAT_ROWS, head_size), jnp.bfloat16),
    )(flags, gathered_q, keys, values)


def layer(
    query,
    suffix_kv,
    segment_ids,
    request_prefix,
    prefix_kv,
    shard_prefix,
    residual,
    out_weight,
    norm_gain,
    expert_ids,
    gate_weights,
    expert_in,
    expert_out,
):
    tok_rows = query.shape[0]
    head_size = suffix_kv.shape[3]
    heads_here = query.shape[1] // head_size
    kv_head = lax.axis_index("tensor") * heads_here // (QH // KVH)
    score_scale = head_size ** (-0.5)
    queries = query.reshape(tok_rows, heads_here, head_size)
    segments = segment_ids[0]
    requests = jnp.arange(request_prefix.shape[1], dtype=jnp.int32)
    row_prefix = jnp.sum(
        jnp.where(segments[:, None] == requests[None, :], request_prefix[0][None, :], 0), axis=1
    )
    prefix_row = jnp.zeros((1, head_size), jnp.bfloat16).at[0, :tok_rows].set(
        row_prefix.astype(jnp.bfloat16)
    )
    sources = lax.axis_size("seq")
    own_cache = lax.dynamic_slice_in_dim(prefix_kv, kv_head, 1, 1)[:, 0]
    got_o, got_shift, got_total = [], [], []
    flags = None
    for head in range(heads_here):
        own_rows = jnp.concatenate(
            [query[:, head * head_size : (head + 1) * head_size], prefix_row], axis=0
        )
        if head == 0:
            gathered_q = lax.all_to_all(
                jnp.broadcast_to(own_rows[None], (sources,) + own_rows.shape),
                "seq", split_axis=0, concat_axis=0, tiled=True,
            )
        else:
            gathered_q = lax.all_gather(own_rows, "seq", axis=0, tiled=False)
        if flags is None:
            valid = gathered_q[:, tok_rows, :tok_rows] == shard_prefix[0].astype(jnp.bfloat16)
            flags = jnp.concatenate(
                [jnp.any(valid, axis=1).astype(jnp.int32), shard_prefix.astype(jnp.int32)]
            )
        outgoing = shard_attention(flags, gathered_q, own_cache[:, 0], own_cache[:, 1], score_scale)
        returned = lax.all_to_all(
            outgoing, "seq", split_axis=0, concat_axis=0, tiled=True
        )
        got_st = returned[:, 0, tok_rows:, :].astype(jnp.float32)
        got_o.append(returned[:, 0, :tok_rows, :].astype(jnp.float32))
        got_shift.append(got_st[:, 0] + got_st[:, 1] + got_st[:, 2])
        got_total.append(got_st[:, 3] + got_st[:, 4] + got_st[:, 5])
    got_o = jnp.stack(got_o, axis=1)
    got_shift = jnp.stack(got_shift, axis=1)
    got_total = jnp.stack(got_total, axis=1)

    own_suffix = lax.dynamic_slice_in_dim(suffix_kv, kv_head, 1, 1).reshape(tok_rows, 2, head_size)
    positions = jnp.arange(tok_rows)
    causal = (segments[:, None] == segments[None, :]) & (positions[None, :] <= positions[:, None])
    suf_scores = (
        jnp.einsum("rhd,kd->hrk", queries, own_suffix[:, 0], preferred_element_type=jnp.float32)
        * score_scale
    )
    suf_scores = jnp.where(causal[None], suf_scores, -jnp.inf)
    suf_shift = jnp.max(suf_scores, axis=2)
    suf_weights = jnp.exp(suf_scores - suf_shift[:, :, None])
    suf_total = jnp.sum(suf_weights, axis=2)
    suf_o = jnp.einsum(
        "hrk,kd->hrd", suf_weights.astype(jnp.bfloat16), own_suffix[:, 1],
        preferred_element_type=jnp.float32,
    )
    common = jnp.maximum(suf_shift, jnp.max(got_shift, axis=0))
    got_scale = jnp.exp(got_shift - common[None])
    suf_scale = jnp.exp(suf_shift - common)
    numer = jnp.sum(got_o * got_scale[..., None], axis=0) + suf_o * suf_scale[..., None]
    denom = jnp.sum(got_total * got_scale, axis=0) + suf_total * suf_scale
    attention = (
        jnp.transpose(numer / denom[..., None], (1, 0, 2))
        .reshape(tok_rows, heads_here * head_size)
        .astype(jnp.bfloat16)
    )
    projected = jnp.dot(attention, out_weight, preferred_element_type=jnp.float32)
    model_width = residual.shape[1]
    slice_width = model_width // lax.axis_size("tensor")
    first_col = lax.axis_index("tensor") * slice_width
    tensor_size = lax.axis_size("tensor")
    shared = jnp.sum(
        lax.all_to_all(
            projected.reshape(tok_rows, tensor_size, slice_width),
            "tensor", split_axis=1, concat_axis=1, tiled=True,
        ),
        axis=1,
    )
    hidden_state = (
        lax.dynamic_slice_in_dim(residual, first_col, slice_width, 1).astype(jnp.float32) + shared
    )
    attended = hidden_state.astype(jnp.bfloat16)
    exp_here = expert_in.shape[0]
    sources = lax.axis_size("seq")
    experts = exp_here * sources
    top_k = expert_ids.shape[1]
    capacity = 2 * tok_rows * top_k // experts
    flat_ids = expert_ids.reshape(-1)
    onehot = (flat_ids[:, None] == jnp.arange(experts, dtype=jnp.int32)[None, :]).astype(jnp.int32)
    slot_index = jnp.sum((jnp.cumsum(onehot, axis=0) - 1) * onehot, axis=1)
    places = flat_ids * capacity + slot_index
    pick = places[:, None] == jnp.arange(experts * capacity, dtype=jnp.int32)[None, :]
    send_pick = jnp.any(pick.reshape(tok_rows, top_k, -1), axis=1).astype(jnp.bfloat16)
    outgoing = lax.dot_general(
        send_pick, attended, (((0,), (0,)), ((), ())), preferred_element_type=jnp.float32
    ).astype(jnp.bfloat16)
    incoming = lax.all_to_all(
        outgoing.reshape(sources, exp_here, capacity, slice_width),
        "seq",
        split_axis=0,
        concat_axis=0,
        tiled=True,
    )
    rows_in = lax.all_gather(incoming, "tensor", axis=3, tiled=True).astype(jnp.float32)
    mean_square = jnp.mean(rows_in * rows_in, axis=3, keepdims=True)
    normed = (rows_in * lax.rsqrt(mean_square + 1e-06) * norm_gain).astype(jnp.bfloat16)
    gate_up = jnp.einsum(
        "sjcd,jdgh->sjcgh",
        normed,
        expert_in,
        preferred_element_type=jnp.float32,
    )
    hidden = (jax.nn.silu(gate_up[:, :, :, 0]) * gate_up[:, :, :, 1]).astype(jnp.bfloat16)
    group_terms = jnp.einsum(
        "sjch,jhd->sjcd", hidden, expert_out, preferred_element_type=jnp.float32
    )
    expert_rows_out = lax.psum_scatter(
        group_terms.astype(jnp.bfloat16), "tensor", scatter_dimension=3, tiled=True
    )
    returned = lax.all_to_all(expert_rows_out, "seq", split_axis=0, concat_axis=0, tiled=True)
    picked = jnp.dot(
        pick.astype(jnp.bfloat16),
        returned.reshape(experts * capacity, slice_width),
        preferred_element_type=jnp.float32,
    ).reshape(tok_rows, top_k, slice_width)
    mixture = jnp.sum(gate_weights[:, :, None] * picked, axis=1)
    layer_out = (hidden_state + mixture).astype(jnp.bfloat16)
    return (attended, layer_out)


def solution(mesh):
    in_specs = (
        P("seq", "tensor"),
        P("seq", None, None, None),
        P("seq", None),
        P("seq", None),
        P("seq", None, None, None),
        P("seq"),
        P("seq", None),
        P("tensor", None),
        P(),
        P("seq", None),
        P("seq", None),
        P("seq", None, None, "tensor"),
        P("seq", "tensor", None),
    )
    out_specs = (P("seq", "tensor"), P("seq", "tensor"))
    return jax.shard_map(layer, mesh=mesh, in_specs=in_specs, out_specs=out_specs, check_vma=False)
```

profile of v0, /device:TPU:32, one launch (start us, length us, event | category | flops | bytes accessed | tf_op | source)
XLA Modules:
  0.0 387.6 jit_solution(16181185770265252293)
XLA Ops:
  9.5 1.2 broadcast_in_dim.31
  10.7 11.4 %all-to-all-start = ((bf16[32,129,128]{2,1,0:T(8,128)(2,1)}), bf16[32,129,128]{2,1,0:T(8,128)(2,1)}, u32[]{:S(2)}, u32[]{:S(2)}) async-start(bf16[32,129,128]{2,1,0:T(8,128)(2,1)} %broadcast_in_dim.31), calls=%async_computation | async-start | bytes 2228224 | tf_op jit(solution)/shard_map/all_to_all | solution.py:129
  23.5 1.4 constant_dynamic-slice_fusion.1
  25.8 26.6 %all-to-all-done.q_ref = bf16[32,129,128]{2,1,0:T(8,128)(2,1)} async-done(((bf16[32,129,128]{2,1,0:T(8,128)(2,1)}), bf16[32,129,128]{2,1,0:T(8,128)(2,1)}, u32[]{:S(2)}, u32[]{:S(2)}) %all-to-all-start) | async-done | bytes 1056800 | tf_op jit(solution)/shard_map/all_to_all | solution.py:129
  52.4 1.5 compare_reduce_fusion
  54.5 48.7 %all-gather.7.cloned.1.call-done.q_ref = bf16[32,129,128]{2,1,0:T(8,128)(2,1)} async-done(((bf16[1,129,128]{2,1,0:T(8,128)(2,1)}), bf16[32,129,128]{2,1,0:T(8,128)(2,1)}) %all-gather.7.cloned.1.call-update) | async-done | bytes 1056784 | tf_op jit(solution)/shard_map/all_gather | solution.py:134
  103.2 17.2 %shard_map.141 = bf16[32,1,144,128]{3,2,1,0:T(8,128)(2,1)} custom-call(s32[33]{0:T(128)} %pad_add_fusion.flag_ref, bf16[32,129,128]{2,1,0:T(8,128)(2,1)} %all-gather.7.cloned.1.call-done.q_ref, bf16[1024,128]{1,0:T(8,128)(2,1)} %get-tuple-element.19.k_ref, bf16[1024,128]{1,0:T(8,128)(2,1)} %get-tuple-element.18.v_ref), custom_call_target="tpu_custom_call" | custom-call | tf_op jit(solution)/shard_map/pallas_call | solution.py:84
  120.5 5.9 %all-to-all-start.2 = ((bf16[32,1,144,128]{3,2,1,0:T(8,128)(2,1)}), bf16[32,1,144,128]{3,2,1,0:T(8,128)(2,1)}, u32[]{:S(2)}, u32[]{:S(2)}) async-start(bf16[32,1,144,128]{3,2,1,0:T(8,128)(2,1)} %shard_map.141), calls=%async_computation.2 | async-start | bytes 2359296 | tf_op jit(solution)/shard_map/all_to_all | solution.py:141
  126.4 17.2 %shard_map.140 = bf16[32,1,144,128]{3,2,1,0:T(8,128)(2,1)} custom-call(s32[33]{0:T(128)} %pad_add_fusion.flag_ref, bf16[32,129,128]{2,1,0:T(8,128)(2,1)} %all-to-all-done.q_ref, bf16[1024,128]{1,0:T(8,128)(2,1)} %get-tuple-element.19.k_ref, bf16[1024,128]{1,0:T(8,128)(2,1)} %get-tuple-element.18.v_ref), custom_call_target="tpu_custom_call" | custom-call | tf_op jit(solution)/shard_map/pallas_call | solution.py:84
  143.6 9.2 %all-to-all-done.2 = bf16[32,1,144,128]{3,2,1,0:T(8,128)(2,1)} async-done(((bf16[32,1,144,128]{3,2,1,0:T(8,128)(2,1)}), bf16[32,1,144,128]{3,2,1,0:T(8,128)(2,1)}, u32[]{:S(2)}, u32[]{:S(2)}) %all-to-all-start.2) | async-done | bytes 1179680 | tf_op jit(solution)/shard_map/all_to_all | solution.py:141
  152.9 5.1 %all-to-all-start.1 = ((bf16[32,1,144,128]{3,2,1,0:T(8,128)(2,1)}), bf16[32,1,144,128]{3,2,1,0:T(8,128)(2,1)}, u32[]{:S(2)}, u32[]{:S(2)}) async-start(bf16[32,1,144,128]{3,2,1,0:T(8,128)(2,1)} %shard_map.140), calls=%async_computation.1 | async-start | bytes 2359296 | tf_op jit(solution)/shard_map/all_to_all | solution.py:141
  158.9 2.3 copy.131
  161.5 0.9 fusion.37
  162.5 21.3 %all-to-all-done.1 = bf16[32,1,144,128]{3,2,1,0:T(8,128)(2,1)} async-done(((bf16[32,1,144,128]{3,2,1,0:T(8,128)(2,1)}), bf16[32,1,144,128]{3,2,1,0:T(8,128)(2,1)}, u32[]{:S(2)}, u32[]{:S(2)}) %all-to-all-start.1) | async-done | bytes 1179680 | tf_op jit(solution)/shard_map/all_to_all | solution.py:141
  184.9 1.3 slice.128
  186.2 1.3 slice.127
  187.5 1.2 multiply_reduce_fusion
  189.1 2.7 fusion.56
  191.8 4.3 %all-to-all-start.3 = ((f32[128,8,256]{2,0,1:T(8,128)}), f32[128,8,256]{2,0,1:T(8,128)}, u32[]{:S(2)}, u32[]{:S(2)}) async-start(f32[128,8,256]{2,0,1:T(8,128)} %fusion.56), calls=%async_computation.3 | async-start | bytes 2097152 | tf_op jit(solution)/shard_map/all_to_all | solution.py:183
  196.6 1.8 reduce-window.6
  199.9 12.3 %all-to-all-done.3 = f32[128,8,256]{2,0,1:T(8,128)} async-done(((f32[128,8,256]{2,0,1:T(8,128)}), f32[128,8,256]{2,0,1:T(8,128)}, u32[]{:S(2)}, u32[]{:S(2)}) %all-to-all-start.3) | async-done | bytes 1048608 | tf_op jit(solution)/shard_map/all_to_all | solution.py:183
  212.1 1.3 reduce_sum.87
  214.7 27.9 %all_to_all.30 = bf16[32,2,24,256]{3,2,1,0:T(8,128)(2,1)} all-to-all(bf16[32,2,24,256]{3,2,1,0:T(8,128)(2,1)S(1)} %bitcast.148), channel_id=1, replica_groups=mesh['seq'=32,'tensor'=8] {'seq'}, dimensions={0} | all-to-all | bytes 1572864 | tf_op jit(solution)/shard_map/all_to_all | solution.py:207
  242.9 41.2 %all-gather.5.cloned.1.call-done = bf16[32,2,24,2048]{3,2,1,0:T(8,128)(2,1)} async-done(((bf16[32,2,24,256]{3,2,1,0:T(8,128)(2,1)}), bf16[32,2,24,2048]{3,2,1,0:T(8,128)(2,1)}) %all-gather.5.cloned.1.call-update) | async-done | bytes 6291472 | tf_op jit(solution)/shard_map/all_gather | solution.py:214
  284.1 4.1 %fusion = f32[32,2,24]{2,1,0:T(2,128)S(1)} fusion(bf16[32,2,24,2048]{3,2,1,0:T(8,128)(2,1)} %all-gather.5.cloned.1.call-done), kind=kLoop, calls=%fused_computation.2 | loop fusion | flops 9435648 | bytes 6297600 | tf_op jit(solution)/shard_map/reduce_sum | solution.py:215
  288.4 5.8 %fusion.12 = f32[32,2,24,2,176]{4,2,3,0,1:T(8,128)S(1)} fusion(bf16[2,2048,2,176]{1,3,2,0:T(8,128)(2,1)S(1)} %copy-done, bf16[32,2,24,2048]{3,2,1,0:T(8,128)(2,1)} %all-gather.5.cloned.1.call-done, f32[2048]{0:T(1024)S(1)} %copy-done.6, f32[32,2,24]{2,1,0:T(2,128)S(1)} %copy.119), kind=kOutput, calls=%fused_computation.18 | convolution fusion | flops 2227175424 | bytes 11352064 | tf_op jit(solution)/shard_map/sjcd,jdgh->sjcgh/dot_general | solution.py:217
  294.2 4.6 %convert_bitcast_fusion = bf16[32,2,24,2048]{3,2,0,1:T(8,128)(2,1)} fusion(bf16[2,176,2048]{2,1,0:T(8,128)(2,1)S(1)} %copy-done.5, f32[32,2,24,2,176]{4,2,3,0,1:T(8,128)S(1)} %fusion.12), kind=kOutput, calls=%fused_computation.8 | convolution fusion | flops 1112064000 | bytes 9895936 | tf_op jit(solution)/shard_map/sjch,jhd->sjcd/dot_general | solution.py:224
  298.8 46.1 %reduce-scatter.2.cloned.1.call-done = bf16[32,2,24,256]{3,2,0,1:T(8,128)(2,1)} async-done(((bf16[32,2,24,2048]{3,2,0,1:T(8,128)(2,1)}), bf16[32,2,24,256]{3,2,0,1:T(8,128)(2,1)}) %reduce-scatter.2.cloned.1.call-update) | async-done | bytes 786448 | tf_op jit(solution)/shard_map/reduce_scatter | solution.py:227
  344.9 1.2 copy.122
  346.1 32.5 %all_to_all.31 = bf16[32,2,24,256]{3,2,1,0:T(8,128)(2,1)S(1)} all-to-all(bf16[32,2,24,256]{3,2,1,0:T(8,128)(2,1)S(1)} %copy.122), channel_id=1, replica_groups=mesh['seq'=32,'tensor'=8] {'seq'}, dimensions={0} | all-to-all | bytes 1572864 | tf_op jit(solution)/shard_map/all_to_all | solution.py:230
  378.6 1.0 fusion.23
  379.6 1.5 add_convert_fusion
  (60 shorter events, 10.9 us)
Async XLA Ops:
  7.2 281.2 %copy-start = (bf16[2,2048,2,176]{1,3,2,0:T(8,128)(2,1)S(1)}, bf16[2,2048,2,176]{1,3,2,0:T(8,128)(2,1)}, u32[]{:S(2)}) copy-start(bf16[2,2048,2,176]{1,3,2,0:T(8,128)(2,1)} %param.26) | copy-start | bytes 8650756
  10.7 41.7 %all-to-all-start = ((bf16[32,129,128]{2,1,0:T(8,128)(2,1)}), bf16[32,129,128]{2,1,0:T(8,128)(2,1)}, u32[]{:S(2)}, u32[]{:S(2)}) async-start(bf16[32,129,128]{2,1,0:T(8,128)(2,1)} %broadcast_in_dim.31), calls=%async_computation | async-start | bytes 2228224 | tf_op jit(solution)/shard_map/all_to_all | solution.py:129
  22.1 81.1 %all-gather.7.cloned.1.call-start = ((), (), s32[]{:S(2)}) async-start(), calls=%async_computation.9 | async-start | bytes 1148928 | tf_op jit(solution)/shard_map/all_gather | solution.py:134
  120.5 32.4 %all-to-all-start.2 = ((bf16[32,1,144,128]{3,2,1,0:T(8,128)(2,1)}), bf16[32,1,144,128]{3,2,1,0:T(8,128)(2,1)}, u32[]{:S(2)}, u32[]{:S(2)}) async-start(bf16[32,1,144,128]{3,2,1,0:T(8,128)(2,1)} %shard_map.141), calls=%async_computation.2 | async-start | bytes 2359296 | tf_op jit(solution)/shard_map/all_to_all | solution.py:141
  143.6 17.5 %copy-start.4 = (s32[1,128]{1,0:T(1,128)S(1)}, s32[1,128]{1,0:T(1,128)}, u32[]{:S(2)}) copy-start(s32[1,128]{1,0:T(1,128)} %param.17) | copy-start | bytes 1540
  143.6 17.6 %copy-start.2 = (bf16[128,256]{1,0:T(8,128)(2,1)S(1)}, bf16[128,256]{1,0:T(8,128)(2,1)}, u32[]{:S(2)}) copy-start(bf16[128,256]{1,0:T(8,128)(2,1)} %param.15) | copy-start | bytes 196612
  152.9 30.9 %all-to-all-start.1 = ((bf16[32,1,144,128]{3,2,1,0:T(8,128)(2,1)}), bf16[32,1,144,128]{3,2,1,0:T(8,128)(2,1)}, u32[]{:S(2)}, u32[]{:S(2)}) async-start(bf16[32,1,144,128]{3,2,1,0:T(8,128)(2,1)} %shard_map.140), calls=%async_computation.1 | async-start | bytes 2359296 | tf_op jit(solution)/shard_map/all_to_all | solution.py:141
  188.8 7.4 %copy-start.3 = (s32[128,6]{0,1:T(8,128)S(1)}, s32[128,6]{0,1:T(8,128)}, u32[]{:S(2)}) copy-start(s32[128,6]{0,1:T(8,128)} %param.24) | copy-start | bytes 9220
  191.8 20.3 %all-to-all-start.3 = ((f32[128,8,256]{2,0,1:T(8,128)}), f32[128,8,256]{2,0,1:T(8,128)}, u32[]{:S(2)}, u32[]{:S(2)}) async-start(f32[128,8,256]{2,0,1:T(8,128)} %fusion.56), calls=%async_computation.3 | async-start | bytes 2097152 | tf_op jit(solution)/shard_map/all_to_all | solution.py:183
  196.1 88.0 %all-gather.5.cloned.1.call-start = ((), (), s32[]{:S(2)}) async-start(), calls=%async_computation.7 | async-start | bytes 7077888 | tf_op jit(solution)/shard_map/all_gather | solution.py:214
  214.3 73.9 %copy-start.1 = (bf16[128,256]{1,0:T(8,128)(2,1)}, bf16[128,256]{1,0:T(8,128)(2,1)S(1)}, u32[]{:S(2)}) copy-start(bf16[128,256]{1,0:T(8,128)(2,1)S(1)} %fusion.41) | copy-start | bytes 196612
  242.7 45.7 %copy-start.6 = (f32[2048]{0:T(1024)S(1)}, f32[2048]{0:T(1024)}, u32[]{:S(2)}) copy-start(f32[2048]{0:T(1024)} %param.23) | copy-start | bytes 24580
  242.7 102.2 %reduce-scatter.2.cloned.1.call-start = ((), (), s32[]{:S(2)}) async-start(), calls=%async_computation.8 | async-start | bytes 7077888 | tf_op jit(solution)/shard_map/reduce_scatter | solution.py:227
  288.4 5.8 %copy-start.5 = (bf16[2,176,2048]{2,1,0:T(8,128)(2,1)S(1)}, bf16[2,176,2048]{2,1,0:T(8,128)(2,1)}, u32[]{:S(2)}) copy-start(bf16[2,176,2048]{2,1,0:T(8,128)(2,1)} %param.27) | copy-start | bytes 4325380
  298.8 79.9 %copy-start.7 = (f32[128,6]{0,1:T(8,128)S(1)}, f32[128,6]{0,1:T(8,128)}, u32[]{:S(2)}) copy-start(f32[128,6]{0,1:T(8,128)} %param.25) | copy-start | bytes 9220
Sparse Core Ops, SparseCore 0:
  26.1 77.0 all-gather.6
  242.8 41.2 all-gather.4
  298.9 45.9 reduce-scatter.1
where the time goes:
time: 389 us; the launch traced here: 388 us
  waiting for transfers between devices  206 us (53%)
  blocking collectives  60.4 us (16%)
  Pallas kernels  34.5 us (9%)
  starting transfers between devices  27 us (7%)
  other arithmetic  17.7 us (5%)
  matrix products  14.8 us (4%)
  between operations  14.7 us (4%)
  local copies, waits for them, and re-layouts  12.4 us (3%)
    all_gather x1, waiting for transfers between devices, layer(): gathered_q = lax.all_gather(own_rows, 'seq', axis=0, tiled=False)  48.7 us
    reduce_scatter x1, waiting for transfers between devices, layer(): lax.psum_scatter(group_terms.astype(jnp.bfloat16), 'tensor', scatter_dime...  46.1 us
    all_gather x1, waiting for transfers between devices, layer(): lax.all_gather(incoming, 'tensor', axis=3, tiled=True).astype(jnp.float32)  41.2 us
    pallas_call x2, Pallas kernels, shard_attention(): pl.pallas_call(kernel, grid_spec=grid_spec, out_shape=jax.ShapeDtypeStruc...  34.5 us
    all_to_all x1, blocking collectives, layer(): lax.all_to_all(expert_rows_out, 'seq', split_axis=0, concat_axis=0, tiled...  32.5 us
    all_to_all x2, waiting for transfers between devices, layer(): lax.all_to_all(outgoing, 'seq', split_axis=0, concat_axis=0, tiled=True)  30.5 us
    all_to_all x1, blocking collectives, layer(): lax.all_to_all(outgoing.reshape(sources, exp_here, capacity, slice_width)...  27.9 us
    all_to_all x1, waiting for transfers between devices, layer(): lax.all_to_all(jnp.broadcast_to(own_rows[None], (sources,) + own_rows.sha...  26.6 us
  transfers between devices with their start and end apart: 7, of which 7 were waited for; matrix products, arithmetic and copies ran while one was open for 3% of the time, Pallas kernels for 4%

commit v1 on v0

--- a/solution.py
+++ b/solution.py
@@ -119,19 +119,31 @@
     )
     sources = lax.axis_size("seq")
     own_cache = lax.dynamic_slice_in_dim(prefix_kv, kv_head, 1, 1)[:, 0]
-    got_o, got_shift, got_total = [], [], []
+    own_suffix = lax.dynamic_slice_in_dim(suffix_kv, kv_head, 1, 1).reshape(tok_rows, 2, head_size)
+    positions = jnp.arange(tok_rows)
+    causal = (segments[:, None] == segments[None, :]) & (positions[None, :] <= positions[:, None])
+    suf_scores = (
+        jnp.einsum("rhd,kd->hrk", queries, own_suffix[:, 0], preferred_element_type=jnp.float32)
+        * score_scale
+    )
+    suf_scores = jnp.where(causal[None], suf_scores, -jnp.inf)
+    suf_shift = jnp.max(suf_scores, axis=2)
+    suf_weights = jnp.exp(suf_scores - suf_shift[:, :, None])
+    suf_total = jnp.sum(suf_weights, axis=2)
+    suf_o = jnp.einsum(
+        "hrk,kd->hrd", suf_weights.astype(jnp.bfloat16), own_suffix[:, 1],
+        preferred_element_type=jnp.float32,
+    )
+    projected = None
     flags = None
     for head in range(heads_here):
         own_rows = jnp.concatenate(
             [query[:, head * head_size : (head + 1) * head_size], prefix_row], axis=0
         )
-        if head == 0:
-            gathered_q = lax.all_to_all(
-                jnp.broadcast_to(own_rows[None], (sources,) + own_rows.shape),
-                "seq", split_axis=0, concat_axis=0, tiled=True,
-            )
-        else:
-            gathered_q = lax.all_gather(own_rows, "seq", axis=0, tiled=False)
+        gathered_q = lax.all_to_all(
+            jnp.broadcast_to(own_rows[None], (sources,) + own_rows.shape),
+            "seq", split_axis=0, concat_axis=0, tiled=True,
+        )
         if flags is None:
             valid = gathered_q[:, tok_rows, :tok_rows] == shard_prefix[0].astype(jnp.bfloat16)
             flags = jnp.concatenate(
@@ -142,48 +154,30 @@
             outgoing, "seq", split_axis=0, concat_axis=0, tiled=True
         )
         got_st = returned[:, 0, tok_rows:, :].astype(jnp.float32)
-        got_o.append(returned[:, 0, :tok_rows, :].astype(jnp.float32))
-        got_shift.append(got_st[:, 0] + got_st[:, 1] + got_st[:, 2])
-        got_total.append(got_st[:, 3] + got_st[:, 4] + got_st[:, 5])
-    got_o = jnp.stack(got_o, axis=1)
-    got_shift = jnp.stack(got_shift, axis=1)
-    got_total = jnp.stack(got_total, axis=1)
-
-    own_suffix = lax.dynamic_slice_in_dim(suffix_kv, kv_head, 1, 1).reshape(tok_rows, 2, head_size)
-    positions = jnp.arange(tok_rows)
-    causal = (segments[:, None] == segments[None, :]) & (positions[None, :] <= positions[:, None])
-    suf_scores = (
-        jnp.einsum("rhd,kd->hrk", queries, own_suffix[:, 0], preferred_element_type=jnp.float32)
-        * score_scale
-    )
-    suf_scores = jnp.where(causal[None], suf_scores, -jnp.inf)
-    suf_shift = jnp.max(suf_scores, axis=2)
-    suf_weights = jnp.exp(suf_scores - suf_shift[:, :, None])
-    suf_total = jnp.sum(suf_weights, axis=2)
-    suf_o = jnp.einsum(
-        "hrk,kd->hrd", suf_weights.astype(jnp.bfloat16), own_suffix[:, 1],
-        preferred_element_type=jnp.float32,
-    )
-    common = jnp.maximum(suf_shift, jnp.max(got_shift, axis=0))
-    got_scale = jnp.exp(got_shift - common[None])
-    suf_scale = jnp.exp(suf_shift - common)
-    numer = jnp.sum(got_o * got_scale[..., None], axis=0) + suf_o * suf_scale[..., None]
-    denom = jnp.sum(got_total * got_scale, axis=0) + suf_total * suf_scale
-    attention = (
-        jnp.transpose(numer / denom[..., None], (1, 0, 2))
-        .reshape(tok_rows, heads_here * head_size)
-        .astype(jnp.bfloat16)
-    )
-    projected = jnp.dot(attention, out_weight, preferred_element_type=jnp.float32)
+        got_o = returned[:, 0, :tok_rows, :].astype(jnp.float32)
+        got_shift = got_st[:, 0] + got_st[:, 1] + got_st[:, 2]
+        got_total = got_st[:, 3] + got_st[:, 4] + got_st[:, 5]
+        common = jnp.maximum(suf_shift[head], jnp.max(got_shift, axis=0))
+        got_scale = jnp.exp(got_shift - common[None])
+        suf_scale = jnp.exp(suf_shift[head] - common)
+        numer = jnp.sum(got_o * got_scale[..., None], axis=0) + suf_o[head] * suf_scale[:, None]
+        denom = jnp.sum(got_total * got_scale, axis=0) + suf_total[head] * suf_scale
+        attention = (numer / denom[:, None]).astype(jnp.bfloat16)
+        part = jnp.dot(
+            attention,
+            out_weight[head * head_size : (head + 1) * head_size],
+            preferred_element_type=jnp.float32,
+        )
+        projected = part if projected is None else projected + part
     model_width = residual.shape[1]
     slice_width = model_width // lax.axis_size("tensor")
     first_col = lax.axis_index("tensor") * slice_width
     tensor_size = lax.axis_size("tensor")
     shared = jnp.sum(
         lax.all_to_all(
-            projected.reshape(tok_rows, tensor_size, slice_width),
+            projected.astype(jnp.bfloat16).reshape(tok_rows, tensor_size, slice_width),
             "tensor", split_axis=1, concat_axis=1, tiled=True,
-        ),
+        ).astype(jnp.float32),
         axis=1,
     )
     hidden_state = (

time: 389 us -> 369 us (0.949)
  waiting for transfers between devices: 206 us -> 154 us
  blocking collectives: 60.4 us -> 103 us
  starting transfers between devices: 27 us -> 19.6 us
  local copies, waits for them, and re-layouts: 12.4 us -> 8.4 us
    all_gather x1 -> x0, waiting for transfers between devices: 48.7 us -> none  [layer(): gathered_q = lax.all_gather(own_rows, 'seq', axis=0, tiled=False)]
    all_to_all x0 -> x1, blocking collectives: none -> 42.1 us  [layer(): lax.all_to_all(jnp.broadcast_to(own_rows[None], (sources,) + own_rows.sha...]
    all_to_all x1, starting transfers between devices: 11.4 us -> 5.34 us  [layer(): lax.all_to_all(jnp.broadcast_to(own_rows[None], (sources,) + own_rows.sha...]
    all_to_all x2, waiting for transfers between devices: 30.5 us -> 35.3 us  [layer(): lax.all_to_all(outgoing, 'seq', split_axis=0, concat_axis=0, tiled=True)]
    all_to_all x1, waiting for transfers between devices: 12.3 us -> 7.57 us  [layer(): lax.all_to_all(projected.astype(jnp.bfloat16).reshape(tok_rows, tensor_si...]
  transfers between devices with their start and end apart: 7 -> 6, of which waited for: 7 -> 6; matrix products, arithmetic and copies ran while one was open for 3% -> 3% of each run, Pallas kernels for 4% -> 5%
where the time goes in v1:
time: 369 us; the launch traced here: 368 us
  waiting for transfers between devices  154 us (42%)
  blocking collectives  103 us (28%)
  Pallas kernels  34.6 us (9%)
  other arithmetic  19.7 us (5%)
  starting transfers between devices  19.6 us (5%)
  between operations  15.1 us (4%)
  matrix products  13.7 us (4%)
  local copies, waits for them, and re-layouts  8.4 us (2%)
    reduce_scatter x1, waiting for transfers between devices, layer(): lax.psum_scatter(group_terms.astype(jnp.bfloat16), 'tensor', scatter_dime...  46.1 us
    all_to_all x1, blocking collectives, layer(): lax.all_to_all(jnp.broadcast_to(own_rows[None], (sources,) + own_rows.sha...  42.1 us
    all_gather x1, waiting for transfers between devices, layer(): lax.all_gather(incoming, 'tensor', axis=3, tiled=True).astype(jnp.float32)  41.2 us
    all_to_all x2, waiting for transfers between devices, layer(): lax.all_to_all(outgoing, 'seq', split_axis=0, concat_axis=0, tiled=True)  35.3 us
    pallas_call x2, Pallas kernels, shard_attention(): pl.pallas_call(kernel, grid_spec=grid_spec, out_shape=jax.ShapeDtypeStruc...  34.6 us
    all_to_all x1, blocking collectives, layer(): lax.all_to_all(expert_rows_out, 'seq', split_axis=0, concat_axis=0, tiled...  32.5 us
    all_to_all x1, blocking collectives, layer(): lax.all_to_all(outgoing.reshape(sources, exp_here, capacity, slice_width)...  28 us
    all_to_all x1, waiting for transfers between devices, layer(): lax.all_to_all(jnp.broadcast_to(own_rows[None], (sources,) + own_rows.sha...  23.9 us
  transfers between devices with their start and end apart: 6, of which 6 were waited for; matrix products, arithmetic and copies ran while one was open for 3% of the time, Pallas kernels for 5%

profile of v1, /device:TPU:32, one launch (start us, length us, event | category | flops | bytes accessed | tf_op | source)
XLA Modules:
  0.0 367.8 jit_solution(8512822812583311873)
XLA Ops:
  9.0 42.1 %all_to_all.35.q_ref = bf16[32,129,128]{2,1,0:T(8,128)(2,1)} all-to-all(bf16[32,129,128]{2,1,0:T(8,128)(2,1)S(1)} %broadcast_in_dim.33), channel_id=1, replica_groups=mesh['seq'=32,'tensor'=8] {'seq'}, dimensions={0} | all-to-all | bytes 2113536 | tf_op jit(solution)/shard_map/all_to_all | solution.py:143
  51.1 1.2 broadcast_in_dim.36
  52.3 5.3 %all-to-all-start.2 = ((bf16[32,129,128]{2,1,0:T(8,128)(2,1)}), bf16[32,129,128]{2,1,0:T(8,128)(2,1)}, u32[]{:S(2)}, u32[]{:S(2)}) async-start(bf16[32,129,128]{2,1,0:T(8,128)(2,1)} %broadcast_in_dim.36), calls=%async_computation.2 | async-start | bytes 2228224 | tf_op jit(solution)/shard_map/all_to_all | solution.py:143
  58.3 1.4 constant_dynamic-slice_fusion.1
  60.7 1.5 compare_reduce_fusion
  62.8 23.9 %all-to-all-done.2.q_ref = bf16[32,129,128]{2,1,0:T(8,128)(2,1)} async-done(((bf16[32,129,128]{2,1,0:T(8,128)(2,1)}), bf16[32,129,128]{2,1,0:T(8,128)(2,1)}, u32[]{:S(2)}, u32[]{:S(2)}) %all-to-all-start.2) | async-done | bytes 1056800 | tf_op jit(solution)/shard_map/all_to_all | solution.py:143
  86.6 17.2 %shard_map.141 = bf16[32,1,144,128]{3,2,1,0:T(8,128)(2,1)} custom-call(s32[33]{0:T(128)} %pad_add_fusion.flag_ref, bf16[32,129,128]{2,1,0:T(8,128)(2,1)} %all-to-all-done.2.q_ref, bf16[1024,128]{1,0:T(8,128)(2,1)} %get-tuple-element.23.k_ref, bf16[1024,128]{1,0:T(8,128)(2,1)} %get-tuple-element.22.v_ref), custom_call_target="tpu_custom_call" | custom-call | tf_op jit(solution)/shard_map/pallas_call | solution.py:84
  103.9 4.6 %all-to-all-start.3 = ((bf16[32,1,144,128]{3,2,1,0:T(8,128)(2,1)}), bf16[32,1,144,128]{3,2,1,0:T(8,128)(2,1)}, u32[]{:S(2)}, u32[]{:S(2)}) async-start(bf16[32,1,144,128]{3,2,1,0:T(8,128)(2,1)} %shard_map.141), calls=%async_computation.3 | async-start | bytes 2359296 | tf_op jit(solution)/shard_map/all_to_all | solution.py:153
  108.5 17.4 %shard_map.140 = bf16[32,1,144,128]{3,2,1,0:T(8,128)(2,1)} custom-call(s32[33]{0:T(128)} %pad_add_fusion.flag_ref, bf16[32,129,128]{2,1,0:T(8,128)(2,1)} %all_to_all.35.q_ref, bf16[1024,128]{1,0:T(8,128)(2,1)} %get-tuple-element.23.k_ref, bf16[1024,128]{1,0:T(8,128)(2,1)} %get-tuple-element.22.v_ref), custom_call_target="tpu_custom_call" | custom-call | tf_op jit(solution)/shard_map/pallas_call | solution.py:84
  125.8 11.9 %all-to-all-done.3 = bf16[32,1,144,128]{3,2,1,0:T(8,128)(2,1)} async-done(((bf16[32,1,144,128]{3,2,1,0:T(8,128)(2,1)}), bf16[32,1,144,128]{3,2,1,0:T(8,128)(2,1)}, u32[]{:S(2)}, u32[]{:S(2)}) %all-to-all-start.3) | async-done | bytes 1179680 | tf_op jit(solution)/shard_map/all_to_all | solution.py:153
  137.8 5.1 %all-to-all-start.1 = ((bf16[32,1,144,128]{3,2,1,0:T(8,128)(2,1)}), bf16[32,1,144,128]{3,2,1,0:T(8,128)(2,1)}, u32[]{:S(2)}, u32[]{:S(2)}) async-start(bf16[32,1,144,128]{3,2,1,0:T(8,128)(2,1)} %shard_map.140), calls=%async_computation.1 | async-start | bytes 2359296 | tf_op jit(solution)/shard_map/all_to_all | solution.py:153
  144.3 1.8 reduce-window.6
  146.9 0.9 fusion.39
  147.9 23.4 %all-to-all-done.1 = bf16[32,1,144,128]{3,2,1,0:T(8,128)(2,1)} async-done(((bf16[32,1,144,128]{3,2,1,0:T(8,128)(2,1)}), bf16[32,1,144,128]{3,2,1,0:T(8,128)(2,1)}, u32[]{:S(2)}, u32[]{:S(2)}) %all-to-all-start.1) | async-done | bytes 1179680 | tf_op jit(solution)/shard_map/all_to_all | solution.py:153
  171.3 1.0 fusion.40
  172.5 1.7 fusion.14
  174.6 1.7 fusion.13
  177.6 4.3 %all-to-all-start.4 = ((bf16[128,8,256]{2,0,1:T(8,128)(2,1)}), bf16[128,8,256]{2,0,1:T(8,128)(2,1)S(1)}, u32[]{:S(2)}, u32[]{:S(2)}) async-start(bf16[128,8,256]{2,0,1:T(8,128)(2,1)} %bitcast.193), calls=%async_computation.4 | async-start | bytes 1048576 | tf_op jit(solution)/shard_map/all_to_all | solution.py:177
  181.9 1.1 fusion.37
  183.2 1.4 fusion.9
  184.6 7.6 %all-to-all-done.4 = bf16[128,8,256]{2,0,1:T(8,128)(2,1)S(1)} async-done(((bf16[128,8,256]{2,0,1:T(8,128)(2,1)}), bf16[128,8,256]{2,0,1:T(8,128)(2,1)S(1)}, u32[]{:S(2)}, u32[]{:S(2)}) %all-to-all-start.4) | async-done | bytes 524320 | tf_op jit(solution)/shard_map/all_to_all | solution.py:177
  193.1 1.4 convolution_convert_fusion
  194.5 28.0 %all_to_all.36 = bf16[32,2,24,256]{3,2,1,0:T(8,128)(2,1)} all-to-all(bf16[32,2,24,256]{3,2,1,0:T(8,128)(2,1)S(1)} %bitcast.192), channel_id=1, replica_groups=mesh['seq'=32,'tensor'=8] {'seq'}, dimensions={0} | all-to-all | bytes 1572864 | tf_op jit(solution)/shard_map/all_to_all | solution.py:201
  222.8 41.2 %all-gather.2.cloned.1.call-done = bf16[32,2,24,2048]{3,2,1,0:T(8,128)(2,1)} async-done(((bf16[32,2,24,256]{3,2,1,0:T(8,128)(2,1)}), bf16[32,2,24,2048]{3,2,1,0:T(8,128)(2,1)}) %all-gather.2.cloned.1.call-update) | async-done | bytes 6291472 | tf_op jit(solution)/shard_map/all_gather | solution.py:208
  264.0 4.1 %fusion = f32[32,2,24]{2,1,0:T(2,128)S(1)} fusion(bf16[32,2,24,2048]{3,2,1,0:T(8,128)(2,1)} %all-gather.2.cloned.1.call-done), kind=kLoop, calls=%fused_computation.2 | loop fusion | flops 9435648 | bytes 6297600 | tf_op jit(solution)/shard_map/reduce_sum | solution.py:209
  268.3 5.8 %fusion.15 = f32[32,2,24,2,176]{4,2,3,0,1:T(8,128)S(1)} fusion(bf16[2,2048,2,176]{1,3,2,0:T(8,128)(2,1)S(1)} %copy-done, bf16[32,2,24,2048]{3,2,1,0:T(8,128)(2,1)} %all-gather.2.cloned.1.call-done, f32[2048]{0:T(1024)S(1)} %copy-done.8, f32[32,2,24]{2,1,0:T(2,128)S(1)} %copy.123), kind=kOutput, calls=%fused_computation.23 | convolution fusion | flops 2227175424 | bytes 11352064 | tf_op jit(solution)/shard_map/sjcd,jdgh->sjcgh/dot_general | solution.py:211
  274.0 4.6 %convert_bitcast_fusion = bf16[32,2,24,2048]{3,2,0,1:T(8,128)(2,1)} fusion(bf16[2,176,2048]{2,1,0:T(8,128)(2,1)S(1)} %copy-done.7, f32[32,2,24,2,176]{4,2,3,0,1:T(8,128)S(1)} %fusion.15), kind=kOutput, calls=%fused_computation.8 | convolution fusion | flops 1112064000 | bytes 9895936 | tf_op jit(solution)/shard_map/sjch,jhd->sjcd/dot_general | solution.py:218
  278.7 46.1 %reduce-scatter.2.cloned.1.call-done = bf16[32,2,24,256]{3,2,0,1:T(8,128)(2,1)} async-done(((bf16[32,2,24,2048]{3,2,0,1:T(8,128)(2,1)}), bf16[32,2,24,256]{3,2,0,1:T(8,128)(2,1)}) %reduce-scatter.2.cloned.1.call-update) | async-done | bytes 786448 | tf_op jit(solution)/shard_map/reduce_scatter | solution.py:221
  324.8 1.2 copy.126
  326.0 32.5 %all_to_all.37 = bf16[32,2,24,256]{3,2,1,0:T(8,128)(2,1)S(1)} all-to-all(bf16[32,2,24,256]{3,2,1,0:T(8,128)(2,1)S(1)} %copy.126), channel_id=1, replica_groups=mesh['seq'=32,'tensor'=8] {'seq'}, dimensions={0} | all-to-all | bytes 1572864 | tf_op jit(solution)/shard_map/all_to_all | solution.py:224
  358.5 1.0 fusion.26
  359.5 1.5 add_convert_fusion
  (63 shorter events, 8.9 us)
Async XLA Ops:
  7.2 261.1 %copy-start = (bf16[2,2048,2,176]{1,3,2,0:T(8,128)(2,1)S(1)}, bf16[2,2048,2,176]{1,3,2,0:T(8,128)(2,1)}, u32[]{:S(2)}) copy-start(bf16[2,2048,2,176]{1,3,2,0:T(8,128)(2,1)} %param.26) | copy-start | bytes 8650756
  52.3 34.3 %all-to-all-start.2 = ((bf16[32,129,128]{2,1,0:T(8,128)(2,1)}), bf16[32,129,128]{2,1,0:T(8,128)(2,1)}, u32[]{:S(2)}, u32[]{:S(2)}) async-start(bf16[32,129,128]{2,1,0:T(8,128)(2,1)} %broadcast_in_dim.36), calls=%async_computation.2 | async-start | bytes 2228224 | tf_op jit(solution)/shard_map/all_to_all | solution.py:143
  103.9 33.9 %all-to-all-start.3 = ((bf16[32,1,144,128]{3,2,1,0:T(8,128)(2,1)}), bf16[32,1,144,128]{3,2,1,0:T(8,128)(2,1)}, u32[]{:S(2)}, u32[]{:S(2)}) async-start(bf16[32,1,144,128]{3,2,1,0:T(8,128)(2,1)} %shard_map.141), calls=%async_computation.3 | async-start | bytes 2359296 | tf_op jit(solution)/shard_map/all_to_all | solution.py:153
  108.5 34.5 %copy-start.5 = (s32[128,6]{0,1:T(8,128)S(1)}, s32[128,6]{0,1:T(8,128)}, u32[]{:S(2)}) copy-start(s32[128,6]{0,1:T(8,128)} %param.24) | copy-start | bytes 9220
  125.8 20.5 %copy-start.6 = (s32[1,128]{1,0:T(1,128)S(1)}, s32[1,128]{1,0:T(1,128)}, u32[]{:S(2)}) copy-start(s32[1,128]{1,0:T(1,128)} %param.17) | copy-start | bytes 1540
  125.8 20.6 %copy-start.4 = (bf16[128,256]{1,0:T(8,128)(2,1)S(1)}, bf16[128,256]{1,0:T(8,128)(2,1)}, u32[]{:S(2)}) copy-start(bf16[128,256]{1,0:T(8,128)(2,1)} %param.15) | copy-start | bytes 196612
  137.8 33.5 %all-to-all-start.1 = ((bf16[32,1,144,128]{3,2,1,0:T(8,128)(2,1)}), bf16[32,1,144,128]{3,2,1,0:T(8,128)(2,1)}, u32[]{:S(2)}, u32[]{:S(2)}) async-start(bf16[32,1,144,128]{3,2,1,0:T(8,128)(2,1)} %shard_map.140), calls=%async_computation.1 | async-start | bytes 2359296 | tf_op jit(solution)/shard_map/all_to_all | solution.py:153
  146.1 28.6 %copy-start.1 = (s32[64,6,128]{2,0,1:T(8,128)}, s32[64,6,128]{2,0,1:T(8,128)S(1)}, u32[]{:S(2)}) copy-start(s32[64,6,128]{2,0,1:T(8,128)S(1)} %reduce-window.6) | copy-start | bytes 589828
  171.3 3.0 copy-start.2
  177.6 14.6 %all-to-all-start.4 = ((bf16[128,8,256]{2,0,1:T(8,128)(2,1)}), bf16[128,8,256]{2,0,1:T(8,128)(2,1)S(1)}, u32[]{:S(2)}, u32[]{:S(2)}) async-start(bf16[128,8,256]{2,0,1:T(8,128)(2,1)} %bitcast.193), calls=%async_computation.4 | async-start | bytes 1048576 | tf_op jit(solution)/shard_map/all_to_all | solution.py:177
  181.9 82.1 %all-gather.2.cloned.1.call-start = ((), (), s32[]{:S(2)}) async-start(), calls=%async_computation.8 | async-start | bytes 7077888 | tf_op jit(solution)/shard_map/all_gather | solution.py:208
  193.1 74.9 %copy-start.3 = (bf16[128,256]{1,0:T(8,128)(2,1)}, bf16[128,256]{1,0:T(8,128)(2,1)S(1)}, u32[]{:S(2)}) copy-start(bf16[128,256]{1,0:T(8,128)(2,1)S(1)} %fusion.43) | copy-start | bytes 196612
  222.6 45.7 %copy-start.8 = (f32[2048]{0:T(1024)S(1)}, f32[2048]{0:T(1024)}, u32[]{:S(2)}) copy-start(f32[2048]{0:T(1024)} %param.23) | copy-start | bytes 24580
  222.6 102.2 %reduce-scatter.2.cloned.1.call-start = ((), (), s32[]{:S(2)}) async-start(), calls=%async_computation.9 | async-start | bytes 7077888 | tf_op jit(solution)/shard_map/reduce_scatter | solution.py:221
  268.3 5.8 %copy-start.7 = (bf16[2,176,2048]{2,1,0:T(8,128)(2,1)S(1)}, bf16[2,176,2048]{2,1,0:T(8,128)(2,1)}, u32[]{:S(2)}) copy-start(bf16[2,176,2048]{2,1,0:T(8,128)(2,1)} %param.27) | copy-start | bytes 4325380
  278.6 79.9 %copy-start.9 = (f32[128,6]{0,1:T(8,128)S(1)}, f32[128,6]{0,1:T(8,128)}, u32[]{:S(2)}) copy-start(f32[128,6]{0,1:T(8,128)} %param.25) | copy-start | bytes 9220
Sparse Core Ops, SparseCore 0:
  222.7 41.2 all-gather.1
  278.8 45.9 reduce-scatter.1

commit v2 on v1

--- a/solution.py
+++ b/solution.py
@@ -25,10 +25,9 @@
     return hi, mid, lo
 
 
-def shard_kernel(flag_ref, q_ref, k_ref, v_ref, o_ref, *, score_scale):
+def shard_kernel(flag_ref, q_ref, p_ref, k_ref, v_ref, o_ref, *, score_scale):
     step = pl.program_id(0)
-    blocks, padded_rows, width = q_ref.shape
-    rows = padded_rows - 1
+    blocks, rows, width = q_ref.shape
     stat_rows = o_ref.shape[2] - rows
     owner = flag_ref[flag_ref.shape[0] - 1].astype(jnp.float32)
     kind = lax.broadcasted_iota(jnp.int32, (stat_rows, width), 0)
@@ -57,7 +56,7 @@
             for col, part in enumerate(split3(shift) + split3(total)):
                 table = jnp.where(lane == col, part, table)
             table = jnp.transpose(table)[:stat_rows, :]
-            matching = q_ref[i, rows:, :].astype(jnp.float32) == owner
+            matching = p_ref[i].astype(jnp.float32) == owner
             o_ref[i, 0, rows:, :] = jnp.where(matching, table, blank).astype(jnp.bfloat16)
 
         @pl.when(jnp.logical_not(present))
@@ -66,16 +65,17 @@
             o_ref[i, 0, rows:, :] = blank.astype(jnp.bfloat16)
 
 
-def shard_attention(flags, gathered_q, keys, values, score_scale):
-    sources, padded_rows, head_size = gathered_q.shape
-    rows = padded_rows - 1
+def shard_attention(flags, gathered_q, prefix_rows, keys, values, score_scale):
+    sources = prefix_rows.shape[0]
+    rows, head_size = gathered_q.shape[1] // 8 * 8, keys.shape[1]
     tb = TOKEN_BLOCKS
     kernel = functools.partial(shard_kernel, score_scale=score_scale)
     grid_spec = pltpu.PrefetchScalarGridSpec(
         num_scalar_prefetch=1,
         grid=(sources // tb,),
         in_specs=[
-            pl.BlockSpec((tb, padded_rows, head_size), lambda b, f: (b, 0, 0)),
+            pl.BlockSpec((tb, rows, head_size), lambda b, f: (b, 0, 0)),
+            pl.BlockSpec((tb, 1, head_size), lambda b, f: (b, 0, 0)),
             pl.BlockSpec(keys.shape, lambda b, f: (0, 0)),
             pl.BlockSpec(values.shape, lambda b, f: (0, 0)),
         ],
@@ -85,7 +85,7 @@
         kernel,
         grid_spec=grid_spec,
         out_shape=jax.ShapeDtypeStruct((sources, 1, rows + STAT_ROWS, head_size), jnp.bfloat16),
-    )(flags, gathered_q, keys, values)
+    )(flags, gathered_q, prefix_rows, keys, values)
 
 
 def layer(
@@ -137,19 +137,22 @@
     projected = None
     flags = None
     for head in range(heads_here):
-        own_rows = jnp.concatenate(
-            [query[:, head * head_size : (head + 1) * head_size], prefix_row], axis=0
-        )
+        own_rows = query[:, head * head_size : (head + 1) * head_size]
+        if head == 0:
+            own_rows = jnp.concatenate([own_rows, prefix_row], axis=0)
         gathered_q = lax.all_to_all(
             jnp.broadcast_to(own_rows[None], (sources,) + own_rows.shape),
             "seq", split_axis=0, concat_axis=0, tiled=True,
         )
         if flags is None:
+            prefix_rows = gathered_q[:, tok_rows:, :]
             valid = gathered_q[:, tok_rows, :tok_rows] == shard_prefix[0].astype(jnp.bfloat16)
             flags = jnp.concatenate(
                 [jnp.any(valid, axis=1).astype(jnp.int32), shard_prefix.astype(jnp.int32)]
             )
-        outgoing = shard_attention(flags, gathered_q, own_cache[:, 0], own_cache[:, 1], score_scale)
+        outgoing = shard_attention(
+            flags, gathered_q, prefix_rows, own_cache[:, 0], own_cache[:, 1], score_scale
+        )
         returned = lax.all_to_all(
             outgoing, "seq", split_axis=0, concat_axis=0, tiled=True
         )

time: 369 us -> 354 us (0.959)
  waiting for transfers between devices: 154 us -> 137 us
    all_to_all x1, waiting for transfers between devices: 23.9 us -> 3.77 us  [layer(): lax.all_to_all(jnp.broadcast_to(own_rows[None], (sources,) + own_rows.sha...]
  transfers between devices with their start and end apart: 6 -> 6, of which waited for: 6 -> 6; matrix products, arithmetic and copies ran while one was open for 3% -> 4% of each run, Pallas kernels for 5% -> 10%
where the time goes in v2:
time: 354 us; the launch traced here: 353 us
  waiting for transfers between devices  137 us (39%)
  blocking collectives  103 us (29%)
  Pallas kernels  34.7 us (10%)
  starting transfers between devices  20.4 us (6%)
  other arithmetic  19.7 us (6%)
  between operations  15.1 us (4%)
  matrix products  13.7 us (4%)
  local copies, waits for them, and re-layouts  9.88 us (3%)
    reduce_scatter x1, waiting for transfers between devices, layer(): lax.psum_scatter(group_terms.astype(jnp.bfloat16), 'tensor', scatter_dime...  46.1 us
    all_to_all x1, blocking collectives, layer(): lax.all_to_all(jnp.broadcast_to(own_rows[None], (sources,) + own_rows.sha...  42.1 us
    all_gather x1, waiting for transfers between devices, layer(): lax.all_gather(incoming, 'tensor', axis=3, tiled=True).astype(jnp.float32)  41.2 us
    all_to_all x2, waiting for transfers between devices, layer(): lax.all_to_all(outgoing, 'seq', split_axis=0, concat_axis=0, tiled=True)  38 us
    pallas_call x2, Pallas kernels, shard_attention(): pl.pallas_call(kernel, grid_spec=grid_spec, out_shape=jax.ShapeDtypeStruc...  34.7 us
    all_to_all x1, blocking collectives, layer(): lax.all_to_all(expert_rows_out, 'seq', split_axis=0, concat_axis=0, tiled...  32.5 us
    all_to_all x1, blocking collectives, layer(): lax.all_to_all(outgoing.reshape(sources, exp_here, capacity, slice_width)...  28.1 us
    all_to_all x2, starting transfers between devices, layer(): lax.all_to_all(outgoing, 'seq', split_axis=0, concat_axis=0, tiled=True)  10.5 us
  transfers between devices with their start and end apart: 6, of which 6 were waited for; matrix products, arithmetic and copies ran while one was open for 4% of the time, Pallas kernels for 10%

profile of v2, /device:TPU:32, one launch (start us, length us, event | category | flops | bytes accessed | tf_op | source)
XLA Modules:
  0.0 352.9 jit_solution(4432714728612602620)
XLA Ops:
  9.0 42.1 %all_to_all.35.q_ref = bf16[32,129,128]{2,1,0:T(8,128)(2,1)} all-to-all(bf16[32,129,128]{2,1,0:T(8,128)(2,1)S(1)} %broadcast_in_dim.33), channel_id=1, replica_groups=mesh['seq'=32,'tensor'=8] {'seq'}, dimensions={0} | all-to-all | bytes 2113536 | tf_op jit(solution)/shard_map/all_to_all | solution.py:143
  51.1 1.2 broadcast_in_dim.36
  52.3 5.3 %all-to-all-start.2 = ((bf16[32,128,128]{2,1,0:T(8,128)(2,1)}), bf16[32,128,128]{2,1,0:T(8,128)(2,1)}, u32[]{:S(2)}, u32[]{:S(2)}) async-start(bf16[32,128,128]{2,1,0:T(8,128)(2,1)} %broadcast_in_dim.36), calls=%async_computation.2 | async-start | bytes 2097152 | tf_op jit(solution)/shard_map/all_to_all | solution.py:143
  58.4 1.4 constant_dynamic-slice_fusion.1
  60.7 1.5 compare_reduce_fusion
  62.2 1.5 slice.159.p_ref
  64.2 17.3 %shard_map.140 = bf16[32,1,144,128]{3,2,1,0:T(8,128)(2,1)} custom-call(s32[33]{0:T(128)} %pad_add_fusion.flag_ref, bf16[32,129,128]{2,1,0:T(8,128)(2,1)} %all_to_all.35.q_ref, bf16[32,1,128]{2,1,0:T(2,128)(2,1)} %slice.159.p_ref, bf16[1024,128]{1,0:T(8,128)(2,1)} %get-tuple-element.23.k_ref, bf16[1024,128]{1,0:T(8,128)(2,1)} %get-tuple-element.22.v_ref), custom_call_target="tpu_custom_call" | custom-call | tf_op jit(solution)/shard_map/pallas_call | solution.py:84
  81.5 3.8 %all-to-all-done.2.q_ref = bf16[32,128,128]{2,1,0:T(8,128)(2,1)} async-done(((bf16[32,128,128]{2,1,0:T(8,128)(2,1)}), bf16[32,128,128]{2,1,0:T(8,128)(2,1)}, u32[]{:S(2)}, u32[]{:S(2)}) %all-to-all-start.2) | async-done | bytes 1048608 | tf_op jit(solution)/shard_map/all_to_all | solution.py:143
  85.3 5.2 %all-to-all-start.1 = ((bf16[32,1,144,128]{3,2,1,0:T(8,128)(2,1)}), bf16[32,1,144,128]{3,2,1,0:T(8,128)(2,1)}, u32[]{:S(2)}, u32[]{:S(2)}) async-start(bf16[32,1,144,128]{3,2,1,0:T(8,128)(2,1)} %shard_map.140), calls=%async_computation.1 | async-start | bytes 2359296 | tf_op jit(solution)/shard_map/all_to_all | solution.py:156
  90.5 17.4 %shard_map.141 = bf16[32,1,144,128]{3,2,1,0:T(8,128)(2,1)} custom-call(s32[33]{0:T(128)} %pad_add_fusion.flag_ref, bf16[32,128,128]{2,1,0:T(8,128)(2,1)} %all-to-all-done.2.q_ref, bf16[32,1,128]{2,1,0:T(2,128)(2,1)} %slice.159.p_ref, bf16[1024,128]{1,0:T(8,128)(2,1)} %get-tuple-element.23.k_ref, bf16[1024,128]{1,0:T(8,128)(2,1)} %get-tuple-element.22.v_ref), custom_call_target="tpu_custom_call" | custom-call | tf_op jit(solution)/shard_map/pallas_call | solution.py:84
  108.0 12.7 %all-to-all-done.1 = bf16[32,1,144,128]{3,2,1,0:T(8,128)(2,1)} async-done(((bf16[32,1,144,128]{3,2,1,0:T(8,128)(2,1)}), bf16[32,1,144,128]{3,2,1,0:T(8,128)(2,1)}, u32[]{:S(2)}, u32[]{:S(2)}) %all-to-all-start.1) | async-done | bytes 1179680 | tf_op jit(solution)/shard_map/all_to_all | solution.py:156
  120.7 5.4 %all-to-all-start.3 = ((bf16[32,1,144,128]{3,2,1,0:T(8,128)(2,1)}), bf16[32,1,144,128]{3,2,1,0:T(8,128)(2,1)}, u32[]{:S(2)}, u32[]{:S(2)}) async-start(bf16[32,1,144,128]{3,2,1,0:T(8,128)(2,1)} %shard_map.141), calls=%async_computation.3 | async-start | bytes 2359296 | tf_op jit(solution)/shard_map/all_to_all | solution.py:156
  127.4 1.8 reduce-window.6
  131.0 25.3 %all-to-all-done.3 = bf16[32,1,144,128]{3,2,1,0:T(8,128)(2,1)} async-done(((bf16[32,1,144,128]{3,2,1,0:T(8,128)(2,1)}), bf16[32,1,144,128]{3,2,1,0:T(8,128)(2,1)}, u32[]{:S(2)}, u32[]{:S(2)}) %all-to-all-start.3) | async-done | bytes 1179680 | tf_op jit(solution)/shard_map/all_to_all | solution.py:156
  156.3 1.0 fusion.39
  157.5 1.7 fusion.14
  159.6 1.7 fusion.13
  162.6 4.3 %all-to-all-start.4 = ((bf16[128,8,256]{2,0,1:T(8,128)(2,1)}), bf16[128,8,256]{2,0,1:T(8,128)(2,1)S(1)}, u32[]{:S(2)}, u32[]{:S(2)}) async-start(bf16[128,8,256]{2,0,1:T(8,128)(2,1)} %bitcast.193), calls=%async_computation.4 | async-start | bytes 1048576 | tf_op jit(solution)/shard_map/all_to_all | solution.py:180
  166.9 1.1 fusion.37
  168.2 1.4 fusion.9
  169.6 7.6 %all-to-all-done.4 = bf16[128,8,256]{2,0,1:T(8,128)(2,1)S(1)} async-done(((bf16[128,8,256]{2,0,1:T(8,128)(2,1)}), bf16[128,8,256]{2,0,1:T(8,128)(2,1)S(1)}, u32[]{:S(2)}, u32[]{:S(2)}) %all-to-all-start.4) | async-done | bytes 524320 | tf_op jit(solution)/shard_map/all_to_all | solution.py:180
  178.1 1.4 convolution_convert_fusion
  179.5 28.1 %all_to_all.36 = bf16[32,2,24,256]{3,2,1,0:T(8,128)(2,1)} all-to-all(bf16[32,2,24,256]{3,2,1,0:T(8,128)(2,1)S(1)} %bitcast.192), channel_id=1, replica_groups=mesh['seq'=32,'tensor'=8] {'seq'}, dimensions={0} | all-to-all | bytes 1572864 | tf_op jit(solution)/shard_map/all_to_all | solution.py:204
  207.9 41.2 %all-gather.2.cloned.1.call-done = bf16[32,2,24,2048]{3,2,1,0:T(8,128)(2,1)} async-done(((bf16[32,2,24,256]{3,2,1,0:T(8,128)(2,1)}), bf16[32,2,24,2048]{3,2,1,0:T(8,128)(2,1)}) %all-gather.2.cloned.1.call-update) | async-done | bytes 6291472 | tf_op jit(solution)/shard_map/all_gather | solution.py:211
  249.0 4.1 %fusion = f32[32,2,24]{2,1,0:T(2,128)S(1)} fusion(bf16[32,2,24,2048]{3,2,1,0:T(8,128)(2,1)} %all-gather.2.cloned.1.call-done), kind=kLoop, calls=%fused_computation.2 | loop fusion | flops 9435648 | bytes 6297600 | tf_op jit(solution)/shard_map/reduce_sum | solution.py:212
  253.4 5.7 %fusion.15 = f32[32,2,24,2,176]{4,2,3,0,1:T(8,128)S(1)} fusion(bf16[2,2048,2,176]{1,3,2,0:T(8,128)(2,1)S(1)} %copy-done, bf16[32,2,24,2048]{3,2,1,0:T(8,128)(2,1)} %all-gather.2.cloned.1.call-done, f32[2048]{0:T(1024)S(1)} %copy-done.8, f32[32,2,24]{2,1,0:T(2,128)S(1)} %copy.123), kind=kOutput, calls=%fused_computation.23 | convolution fusion | flops 2227175424 | bytes 11352064 | tf_op jit(solution)/shard_map/sjcd,jdgh->sjcgh/dot_general | solution.py:214
  259.1 4.6 %convert_bitcast_fusion = bf16[32,2,24,2048]{3,2,0,1:T(8,128)(2,1)} fusion(bf16[2,176,2048]{2,1,0:T(8,128)(2,1)S(1)} %copy-done.7, f32[32,2,24,2,176]{4,2,3,0,1:T(8,128)S(1)} %fusion.15), kind=kOutput, calls=%fused_computation.8 | convolution fusion | flops 1112064000 | bytes 9895936 | tf_op jit(solution)/shard_map/sjch,jhd->sjcd/dot_general | solution.py:221
  263.7 46.1 %reduce-scatter.2.cloned.1.call-done = bf16[32,2,24,256]{3,2,0,1:T(8,128)(2,1)} async-done(((bf16[32,2,24,2048]{3,2,0,1:T(8,128)(2,1)}), bf16[32,2,24,256]{3,2,0,1:T(8,128)(2,1)}) %reduce-scatter.2.cloned.1.call-update) | async-done | bytes 786448 | tf_op jit(solution)/shard_map/reduce_scatter | solution.py:224
  309.9 1.2 copy.126
  311.1 32.5 %all_to_all.37 = bf16[32,2,24,256]{3,2,1,0:T(8,128)(2,1)S(1)} all-to-all(bf16[32,2,24,256]{3,2,1,0:T(8,128)(2,1)S(1)} %copy.126), channel_id=1, replica_groups=mesh['seq'=32,'tensor'=8] {'seq'}, dimensions={0} | all-to-all | bytes 1572864 | tf_op jit(solution)/shard_map/all_to_all | solution.py:227
  343.6 1.0 fusion.26
  344.5 1.5 add_convert_fusion
  (64 shorter events, 9.8 us)
Async XLA Ops:
  7.2 246.2 %copy-start = (bf16[2,2048,2,176]{1,3,2,0:T(8,128)(2,1)S(1)}, bf16[2,2048,2,176]{1,3,2,0:T(8,128)(2,1)}, u32[]{:S(2)}) copy-start(bf16[2,2048,2,176]{1,3,2,0:T(8,128)(2,1)} %param.26) | copy-start | bytes 8650756
  52.3 33.0 %all-to-all-start.2 = ((bf16[32,128,128]{2,1,0:T(8,128)(2,1)}), bf16[32,128,128]{2,1,0:T(8,128)(2,1)}, u32[]{:S(2)}, u32[]{:S(2)}) async-start(bf16[32,128,128]{2,1,0:T(8,128)(2,1)} %broadcast_in_dim.36), calls=%async_computation.2 | async-start | bytes 2097152 | tf_op jit(solution)/shard_map/all_to_all | solution.py:143
  85.3 35.3 %all-to-all-start.1 = ((bf16[32,1,144,128]{3,2,1,0:T(8,128)(2,1)}), bf16[32,1,144,128]{3,2,1,0:T(8,128)(2,1)}, u32[]{:S(2)}, u32[]{:S(2)}) async-start(bf16[32,1,144,128]{3,2,1,0:T(8,128)(2,1)} %shard_map.140), calls=%async_computation.1 | async-start | bytes 2359296 | tf_op jit(solution)/shard_map/all_to_all | solution.py:156
  90.5 35.5 %copy-start.5 = (s32[128,6]{0,1:T(8,128)S(1)}, s32[128,6]{0,1:T(8,128)}, u32[]{:S(2)}) copy-start(s32[128,6]{0,1:T(8,128)} %param.24) | copy-start | bytes 9220
  107.9 21.5 %copy-start.6 = (s32[1,128]{1,0:T(1,128)S(1)}, s32[1,128]{1,0:T(1,128)}, u32[]{:S(2)}) copy-start(s32[1,128]{1,0:T(1,128)} %param.17) | copy-start | bytes 1540
  107.9 21.6 %copy-start.4 = (bf16[128,256]{1,0:T(8,128)(2,1)S(1)}, bf16[128,256]{1,0:T(8,128)(2,1)}, u32[]{:S(2)}) copy-start(bf16[128,256]{1,0:T(8,128)(2,1)} %param.15) | copy-start | bytes 196612
  120.7 35.6 %all-to-all-start.3 = ((bf16[32,1,144,128]{3,2,1,0:T(8,128)(2,1)}), bf16[32,1,144,128]{3,2,1,0:T(8,128)(2,1)}, u32[]{:S(2)}, u32[]{:S(2)}) async-start(bf16[32,1,144,128]{3,2,1,0:T(8,128)(2,1)} %shard_map.141), calls=%async_computation.3 | async-start | bytes 2359296 | tf_op jit(solution)/shard_map/all_to_all | solution.py:156
  129.2 30.5 %copy-start.1 = (s32[64,6,128]{2,0,1:T(8,128)}, s32[64,6,128]{2,0,1:T(8,128)S(1)}, u32[]{:S(2)}) copy-start(s32[64,6,128]{2,0,1:T(8,128)S(1)} %reduce-window.6) | copy-start | bytes 589828
  156.3 3.0 copy-start.2
  162.6 14.6 %all-to-all-start.4 = ((bf16[128,8,256]{2,0,1:T(8,128)(2,1)}), bf16[128,8,256]{2,0,1:T(8,128)(2,1)S(1)}, u32[]{:S(2)}, u32[]{:S(2)}) async-start(bf16[128,8,256]{2,0,1:T(8,128)(2,1)} %bitcast.193), calls=%async_computation.4 | async-start | bytes 1048576 | tf_op jit(solution)/shard_map/all_to_all | solution.py:180
  166.9 82.2 %all-gather.2.cloned.1.call-start = ((), (), s32[]{:S(2)}) async-start(), calls=%async_computation.8 | async-start | bytes 7077888 | tf_op jit(solution)/shard_map/all_gather | solution.py:211
  178.1 75.0 %copy-start.3 = (bf16[128,256]{1,0:T(8,128)(2,1)}, bf16[128,256]{1,0:T(8,128)(2,1)S(1)}, u32[]{:S(2)}) copy-start(bf16[128,256]{1,0:T(8,128)(2,1)S(1)} %fusion.43) | copy-start | bytes 196612
  207.6 45.7 %copy-start.8 = (f32[2048]{0:T(1024)S(1)}, f32[2048]{0:T(1024)}, u32[]{:S(2)}) copy-start(f32[2048]{0:T(1024)} %param.23) | copy-start | bytes 24580
  207.6 102.2 %reduce-scatter.2.cloned.1.call-start = ((), (), s32[]{:S(2)}) async-start(), calls=%async_computation.9 | async-start | bytes 7077888 | tf_op jit(solution)/shard_map/reduce_scatter | solution.py:224
  253.3 5.8 %copy-start.7 = (bf16[2,176,2048]{2,1,0:T(8,128)(2,1)S(1)}, bf16[2,176,2048]{2,1,0:T(8,128)(2,1)}, u32[]{:S(2)}) copy-start(bf16[2,176,2048]{2,1,0:T(8,128)(2,1)} %param.27) | copy-start | bytes 4325380
  263.7 79.9 %copy-start.9 = (f32[128,6]{0,1:T(8,128)S(1)}, f32[128,6]{0,1:T(8,128)}, u32[]{:S(2)}) copy-start(f32[128,6]{0,1:T(8,128)} %param.25) | copy-start | bytes 9220
Sparse Core Ops, SparseCore 0:
  207.7 41.2 all-gather.1
  263.8 45.9 reduce-scatter.1

commit v3 on v2

--- a/solution.py
+++ b/solution.py
@@ -114,8 +114,22 @@
     row_prefix = jnp.sum(
         jnp.where(segments[:, None] == requests[None, :], request_prefix[0][None, :], 0), axis=1
     )
-    prefix_row = jnp.zeros((1, head_size), jnp.bfloat16).at[0, :tok_rows].set(
-        row_prefix.astype(jnp.bfloat16)
+    routing = lax.all_gather(
+        jnp.concatenate([segments, request_prefix[0]]), "seq", axis=0, tiled=False
+    )
+    all_requests = routing[:, tok_rows:]
+    all_prefix = jnp.sum(
+        jnp.where(
+            routing[:, :tok_rows, None] == requests[None, None, :],
+            all_requests[:, None, :],
+            0,
+        ),
+        axis=2,
+    )
+    prefix_rows = all_prefix.astype(jnp.bfloat16)[:, None, :]
+    valid = all_prefix == shard_prefix[0]
+    flags = jnp.concatenate(
+        [jnp.any(valid, axis=1).astype(jnp.int32), shard_prefix.astype(jnp.int32)]
     )
     sources = lax.axis_size("seq")
     own_cache = lax.dynamic_slice_in_dim(prefix_kv, kv_head, 1, 1)[:, 0]
@@ -135,21 +149,12 @@
         preferred_element_type=jnp.float32,
     )
     projected = None
-    flags = None
     for head in range(heads_here):
         own_rows = query[:, head * head_size : (head + 1) * head_size]
-        if head == 0:
-            own_rows = jnp.concatenate([own_rows, prefix_row], axis=0)
         gathered_q = lax.all_to_all(
             jnp.broadcast_to(own_rows[None], (sources,) + own_rows.shape),
             "seq", split_axis=0, concat_axis=0, tiled=True,
         )
-        if flags is None:
-            prefix_rows = gathered_q[:, tok_rows:, :]
-            valid = gathered_q[:, tok_rows, :tok_rows] == shard_prefix[0].astype(jnp.bfloat16)
-            flags = jnp.concatenate(
-                [jnp.any(valid, axis=1).astype(jnp.int32), shard_prefix.astype(jnp.int32)]
-            )
         outgoing = shard_attention(
             flags, gathered_q, prefix_rows, own_cache[:, 0], own_cache[:, 1], score_scale
         )

time: 354 us -> 487 us (1.38)
  blocking collectives: 103 us -> 252 us
  waiting for transfers between devices: 137 us -> 121 us
    unnamed x0 -> x1, blocking collectives: none -> 151 us
    all_to_all x2, waiting for transfers between devices: 38 us -> 26.1 us  [layer(): lax.all_to_all(outgoing, 'seq', split_axis=0, concat_axis=0, tiled=True)]
  transfers between devices with their start and end apart: 6 -> 6, of which waited for: 6 -> 5; matrix products, arithmetic and copies ran while one was open for 4% -> 3% of each run, Pallas kernels for 10% -> 7%
where the time goes in v3:
time: 487 us; the launch traced here: 486 us
  blocking collectives  252 us (52%)
  waiting for transfers between devices  121 us (25%)
  Pallas kernels  34.7 us (7%)
  starting transfers between devices  21.2 us (4%)
  other arithmetic  17.6 us (4%)
  between operations  15.8 us (3%)
  matrix products  13.7 us (3%)
  local copies, waits for them, and re-layouts  10.1 us (2%)
    unnamed x1, blocking collectives  151 us
    reduce_scatter x1, waiting for transfers between devices, layer(): lax.psum_scatter(group_terms.astype(jnp.bfloat16), 'tensor', scatter_dime...  46.1 us
    all_gather x1, waiting for transfers between devices, layer(): lax.all_gather(incoming, 'tensor', axis=3, tiled=True).astype(jnp.float32)  41.2 us
    all_to_all x1, blocking collectives, layer(): lax.all_to_all(jnp.broadcast_to(own_rows[None], (sources,) + own_rows.sha...  39.8 us
    pallas_call x2, Pallas kernels, shard_attention(): pl.pallas_call(kernel, grid_spec=grid_spec, out_shape=jax.ShapeDtypeStruc...  34.7 us
    all_to_all x1, blocking collectives, layer(): lax.all_to_all(expert_rows_out, 'seq', split_axis=0, concat_axis=0, tiled...  32.5 us
    all_to_all x1, blocking collectives, layer(): lax.all_to_all(outgoing.reshape(sources, exp_here, capacity, slice_width)...  27.8 us
    all_to_all x2, waiting for transfers between devices, layer(): lax.all_to_all(outgoing, 'seq', split_axis=0, concat_axis=0, tiled=True)  26.1 us
  transfers between devices with their start and end apart: 6, of which 5 were waited for; matrix products, arithmetic and copies ran while one was open for 3% of the time, Pallas kernels for 7%

profile of v3, /device:TPU:32, one launch (start us, length us, event | category | flops | bytes accessed | tf_op | source)
XLA Modules:
  0.0 485.7 jit_solution(3051479181983046024)
XLA Ops:
  7.2 0.9 fusion.81
  8.3 39.8 %all_to_all.35.q_ref = bf16[32,128,128]{2,1,0:T(8,128)(2,1)} all-to-all(bf16[32,128,128]{2,1,0:T(8,128)(2,1)S(1)} %broadcast_in_dim.33), channel_id=1, replica_groups=mesh['seq'=32,'tensor'=8] {'seq'}, dimensions={0} | all-to-all | bytes 2097152 | tf_op jit(solution)/shard_map/all_to_all | solution.py:154
  48.1 1.2 broadcast_in_dim.30
  49.4 5.3 %all-to-all-start = ((bf16[32,128,128]{2,1,0:T(8,128)(2,1)}), bf16[32,128,128]{2,1,0:T(8,128)(2,1)}, u32[]{:S(2)}, u32[]{:S(2)}) async-start(bf16[32,128,128]{2,1,0:T(8,128)(2,1)} %broadcast_in_dim.30), calls=%async_computation | async-start | bytes 2097152 | tf_op jit(solution)/shard_map/all_to_all | solution.py:154
  56.0 151.4 %all-reduce = s32[4224]{0:T(1024)S(1)} all-reduce(s32[4224]{0:T(1024)S(1)} %add_dynamic-update-slice_fusion), channel_id=2, replica_groups=mesh['seq'=32,'tensor'=8] {'seq'}, use_global_device_ids=true, to_apply=%add | all-reduce | flops 4224 | bytes 33792
  209.2 1.4 constant_dynamic-slice_fusion.1
  212.1 17.3 %shard_map.141 = bf16[32,1,144,128]{3,2,1,0:T(8,128)(2,1)} custom-call(s32[33]{0:T(128)} %pad_add_fusion.flag_ref, bf16[32,128,128]{2,1,0:T(8,128)(2,1)} %all_to_all.35.q_ref, bf16[32,1,128]{2,1,0:T(2,128)(2,1)} %copy.119.p_ref, bf16[1024,128]{1,0:T(8,128)(2,1)} %get-tuple-element.11.k_ref, bf16[1024,128]{1,0:T(8,128)(2,1)} %get-tuple-element.10.v_ref), custom_call_target="tpu_custom_call" | custom-call | tf_op jit(solution)/shard_map/pallas_call | solution.py:84
  229.4 6.1 %all-to-all-start.3 = ((bf16[32,1,144,128]{3,2,1,0:T(8,128)(2,1)}), bf16[32,1,144,128]{3,2,1,0:T(8,128)(2,1)}, u32[]{:S(2)}, u32[]{:S(2)}) async-start(bf16[32,1,144,128]{3,2,1,0:T(8,128)(2,1)} %shard_map.141), calls=%async_computation.3 | async-start | bytes 2359296 | tf_op jit(solution)/shard_map/all_to_all | solution.py:161
  235.5 17.4 %shard_map.140 = bf16[32,1,144,128]{3,2,1,0:T(8,128)(2,1)} custom-call(s32[33]{0:T(128)} %pad_add_fusion.flag_ref, bf16[32,128,128]{2,1,0:T(8,128)(2,1)} %all-to-all-done.q_ref, bf16[32,1,128]{2,1,0:T(2,128)(2,1)} %copy.119.p_ref, bf16[1024,128]{1,0:T(8,128)(2,1)} %get-tuple-element.11.k_ref, bf16[1024,128]{1,0:T(8,128)(2,1)} %get-tuple-element.10.v_ref), custom_call_target="tpu_custom_call" | custom-call | tf_op jit(solution)/shard_map/pallas_call | solution.py:84
  253.0 10.9 %all-to-all-done.3 = bf16[32,1,144,128]{3,2,1,0:T(8,128)(2,1)} async-done(((bf16[32,1,144,128]{3,2,1,0:T(8,128)(2,1)}), bf16[32,1,144,128]{3,2,1,0:T(8,128)(2,1)}, u32[]{:S(2)}, u32[]{:S(2)}) %all-to-all-start.3) | async-done | bytes 1179680 | tf_op jit(solution)/shard_map/all_to_all | solution.py:161
  263.8 5.3 %all-to-all-start.1 = ((bf16[32,1,144,128]{3,2,1,0:T(8,128)(2,1)}), bf16[32,1,144,128]{3,2,1,0:T(8,128)(2,1)}, u32[]{:S(2)}, u32[]{:S(2)}) async-start(bf16[32,1,144,128]{3,2,1,0:T(8,128)(2,1)} %shard_map.140), calls=%async_computation.1 | async-start | bytes 2359296 | tf_op jit(solution)/shard_map/all_to_all | solution.py:161
  270.5 1.8 reduce-window.6
  273.1 0.9 fusion.39
  274.1 15.3 %all-to-all-done.1 = bf16[32,1,144,128]{3,2,1,0:T(8,128)(2,1)} async-done(((bf16[32,1,144,128]{3,2,1,0:T(8,128)(2,1)}), bf16[32,1,144,128]{3,2,1,0:T(8,128)(2,1)}, u32[]{:S(2)}, u32[]{:S(2)}) %all-to-all-start.1) | async-done | bytes 1179680 | tf_op jit(solution)/shard_map/all_to_all | solution.py:161
  289.4 1.0 fusion.40
  290.6 1.7 fusion.14
  292.7 1.7 fusion.13
  295.7 4.3 all-to-all-start.4
  300.0 1.1 fusion.37
  301.3 1.4 fusion.9
  302.7 7.6 %all-to-all-done.4 = bf16[128,8,256]{2,0,1:T(8,128)(2,1)S(1)} async-done(((bf16[128,8,256]{2,0,1:T(8,128)(2,1)}), bf16[128,8,256]{2,0,1:T(8,128)(2,1)S(1)}, u32[]{:S(2)}, u32[]{:S(2)}) %all-to-all-start.4) | async-done | bytes 524320 | tf_op jit(solution)/shard_map/all_to_all | solution.py:185
  311.2 1.4 convolution_convert_fusion
  312.6 27.8 %all_to_all.36 = bf16[32,2,24,256]{3,2,1,0:T(8,128)(2,1)} all-to-all(bf16[32,2,24,256]{3,2,1,0:T(8,128)(2,1)S(1)} %bitcast.194), channel_id=1, replica_groups=mesh['seq'=32,'tensor'=8] {'seq'}, dimensions={0} | all-to-all | bytes 1572864 | tf_op jit(solution)/shard_map/all_to_all | solution.py:209
  340.7 41.2 %all-gather.3.cloned.1.call-done = bf16[32,2,24,2048]{3,2,1,0:T(8,128)(2,1)} async-done(((bf16[32,2,24,256]{3,2,1,0:T(8,128)(2,1)}), bf16[32,2,24,2048]{3,2,1,0:T(8,128)(2,1)}) %all-gather.3.cloned.1.call-update) | async-done | bytes 6291472 | tf_op jit(solution)/shard_map/all_gather | solution.py:216
  381.9 4.1 fusion
  386.2 5.8 %fusion.15 = f32[32,2,24,2,176]{4,2,3,0,1:T(8,128)S(1)} fusion(bf16[2,2048,2,176]{1,3,2,0:T(8,128)(2,1)S(1)} %copy-done, bf16[32,2,24,2048]{3,2,1,0:T(8,128)(2,1)} %all-gather.3.cloned.1.call-done, f32[2048]{0:T(1024)S(1)} %copy-done.9, f32[32,2,24]{2,1,0:T(2,128)S(1)} %copy.136), kind=kOutput, calls=%fused_computation.23 | convolution fusion | flops 2227175424 | bytes 11352064 | tf_op jit(solution)/shard_map/sjcd,jdgh->sjcgh/dot_general | solution.py:219
  392.0 4.6 convert_bitcast_fusion
  396.6 46.1 %reduce-scatter.2.cloned.1.call-done = bf16[32,2,24,256]{3,2,0,1:T(8,128)(2,1)} async-done(((bf16[32,2,24,2048]{3,2,0,1:T(8,128)(2,1)}), bf16[32,2,24,256]{3,2,0,1:T(8,128)(2,1)}) %reduce-scatter.2.cloned.1.call-update) | async-done | bytes 786448 | tf_op jit(solution)/shard_map/reduce_scatter | solution.py:229
  442.7 1.2 copy.139
  443.9 32.5 %all_to_all.37 = bf16[32,2,24,256]{3,2,1,0:T(8,128)(2,1)S(1)} all-to-all(bf16[32,2,24,256]{3,2,1,0:T(8,128)(2,1)S(1)} %copy.139), channel_id=1, replica_groups=mesh['seq'=32,'tensor'=8] {'seq'}, dimensions={0} | all-to-all | bytes 1572864 | tf_op jit(solution)/shard_map/all_to_all | solution.py:232
  476.4 1.0 fusion.26
  477.4 1.5 add_convert_fusion
  (75 shorter events, 9.0 us)
Async XLA Ops:
  7.2 379.0 %copy-start = (bf16[2,2048,2,176]{1,3,2,0:T(8,128)(2,1)S(1)}, bf16[2,2048,2,176]{1,3,2,0:T(8,128)(2,1)}, u32[]{:S(2)}) copy-start(bf16[2,2048,2,176]{1,3,2,0:T(8,128)(2,1)} %param.24) | copy-start | bytes 8650756
  48.1 6.5 %copy-start.11 = (u32[256]{0:T(256)S(1)}, u32[256]{0:T(256)}, u32[]{:S(2)}) copy-start(u32[256]{0:T(256)} %constant.58) | copy-start | bytes 3076
  48.1 7.8 %copy-start.6 = (s32[1,128]{1,0:T(1,128)S(1)}, s32[1,128]{1,0:T(1,128)}, u32[]{:S(2)}) copy-start(s32[1,128]{1,0:T(1,128)} %param.15) | copy-start | bytes 1540
  48.1 7.8 %copy-start.7 = (s32[1,4]{1,0:T(1,128)S(1)}, s32[1,4]{1,0:T(1,128)}, u32[]{:S(2)}) copy-start(s32[1,4]{1,0:T(1,128)} %param.16) | copy-start | bytes 52
  49.4 180.0 %all-to-all-start = ((bf16[32,128,128]{2,1,0:T(8,128)(2,1)}), bf16[32,128,128]{2,1,0:T(8,128)(2,1)}, u32[]{:S(2)}, u32[]{:S(2)}) async-start(bf16[32,128,128]{2,1,0:T(8,128)(2,1)} %broadcast_in_dim.30), calls=%async_computation | async-start | bytes 2097152 | tf_op jit(solution)/shard_map/all_to_all | solution.py:154
  229.4 34.4 %all-to-all-start.3 = ((bf16[32,1,144,128]{3,2,1,0:T(8,128)(2,1)}), bf16[32,1,144,128]{3,2,1,0:T(8,128)(2,1)}, u32[]{:S(2)}, u32[]{:S(2)}) async-start(bf16[32,1,144,128]{3,2,1,0:T(8,128)(2,1)} %shard_map.141), calls=%async_computation.3 | async-start | bytes 2359296 | tf_op jit(solution)/shard_map/all_to_all | solution.py:161
  235.5 33.6 %copy-start.5 = (s32[128,6]{0,1:T(8,128)S(1)}, s32[128,6]{0,1:T(8,128)}, u32[]{:S(2)}) copy-start(s32[128,6]{0,1:T(8,128)} %param.22) | copy-start | bytes 9220
  253.0 19.7 %copy-start.4 = (bf16[128,256]{1,0:T(8,128)(2,1)S(1)}, bf16[128,256]{1,0:T(8,128)(2,1)}, u32[]{:S(2)}) copy-start(bf16[128,256]{1,0:T(8,128)(2,1)} %param.13) | copy-start | bytes 196612
  263.8 25.6 %all-to-all-start.1 = ((bf16[32,1,144,128]{3,2,1,0:T(8,128)(2,1)}), bf16[32,1,144,128]{3,2,1,0:T(8,128)(2,1)}, u32[]{:S(2)}, u32[]{:S(2)}) async-start(bf16[32,1,144,128]{3,2,1,0:T(8,128)(2,1)} %shard_map.140), calls=%async_computation.1 | async-start | bytes 2359296 | tf_op jit(solution)/shard_map/all_to_all | solution.py:161
  272.3 20.5 %copy-start.1 = (s32[64,6,128]{2,0,1:T(8,128)}, s32[64,6,128]{2,0,1:T(8,128)S(1)}, u32[]{:S(2)}) copy-start(s32[64,6,128]{2,0,1:T(8,128)S(1)} %reduce-window.6) | copy-start | bytes 589828
  289.4 3.0 copy-start.2
  295.7 14.6 %all-to-all-start.4 = ((bf16[128,8,256]{2,0,1:T(8,128)(2,1)}), bf16[128,8,256]{2,0,1:T(8,128)(2,1)S(1)}, u32[]{:S(2)}, u32[]{:S(2)}) async-start(bf16[128,8,256]{2,0,1:T(8,128)(2,1)} %bitcast.195), calls=%async_computation.4 | async-start | bytes 1048576 | tf_op jit(solution)/shard_map/all_to_all | solution.py:185
  300.0 81.9 %all-gather.3.cloned.1.call-start = ((), (), s32[]{:S(2)}) async-start(), calls=%async_computation.8 | async-start | bytes 7077888 | tf_op jit(solution)/shard_map/all_gather | solution.py:216
  311.2 74.8 %copy-start.3 = (bf16[128,256]{1,0:T(8,128)(2,1)}, bf16[128,256]{1,0:T(8,128)(2,1)S(1)}, u32[]{:S(2)}) copy-start(bf16[128,256]{1,0:T(8,128)(2,1)S(1)} %fusion.43) | copy-start | bytes 196612
  340.5 45.7 %copy-start.9 = (f32[2048]{0:T(1024)S(1)}, f32[2048]{0:T(1024)}, u32[]{:S(2)}) copy-start(f32[2048]{0:T(1024)} %param.21) | copy-start | bytes 24580
  340.5 102.2 %reduce-scatter.2.cloned.1.call-start = ((), (), s32[]{:S(2)}) async-start(), calls=%async_computation.9 | async-start | bytes 7077888 | tf_op jit(solution)/shard_map/reduce_scatter | solution.py:229
  386.2 5.8 %copy-start.8 = (bf16[2,176,2048]{2,1,0:T(8,128)(2,1)S(1)}, bf16[2,176,2048]{2,1,0:T(8,128)(2,1)}, u32[]{:S(2)}) copy-start(bf16[2,176,2048]{2,1,0:T(8,128)(2,1)} %param.25) | copy-start | bytes 4325380
  396.6 79.9 %copy-start.10 = (f32[128,6]{0,1:T(8,128)S(1)}, f32[128,6]{0,1:T(8,128)}, u32[]{:S(2)}) copy-start(f32[128,6]{0,1:T(8,128)} %param.23) | copy-start | bytes 9220
Sparse Core Ops, SparseCore 0:
  340.6 41.2 all-gather.2
  396.7 45.9 reduce-scatter.1
